TPU v7x, 32 devices: a whole 2x2x4 slice. The times are simulated.
32 devices in a mesh: groups: 2 (over y), row: 4 (over x, core), col: 4 (over z).
Axes of the slice: x: 2, y: 2, z: 4, core: 2. Of those that a mesh axis runs over, the one named last changes fastest.
Arguments:
- tokens: float32 [256, 8192], P(('groups', 'row', 'col')), parts along dimension 0, may hold values from -36 to 36
- modulation: float32 [3, 2, 8192], P(None, 'groups'), parts along dimension 1, may hold values from -4 to 4
- up_weight: float32 [8192, 16384], P('row', 'col'), may hold values from -0.0625 to 0.0625
- up_bias: float32 [16384], P('col'), may hold values from -3 to 3
- down_weight: float32 [16384, 8192], P('col', 'row'), may hold values from -0.046875 to 0.046875
- down_bias: float32 [8192], replicated, may hold values from -3 to 3
Outputs:
- result: float32 [256, 8192], P(('groups', 'row', 'col')), parts along dimension 0
There are 2 independent parts, one for each index of `groups`. A program takes and returns all parts, laid end to end along the dimension named above; an argument that names none is the same for every part. Nothing has to cross between parts.
All inputs are finite; a program needn't handle non-finite values.
Results may differ from a plain program's by a relative error of at most 0.00005.
Values sent between devices are 32-bit elements; how exact they have to be, the bound alone decides.
No kernel may reach another device: no remote copies, remote signals or barrier semaphores. Data moves between devices by JAX's collectives and lax.ppermute only.
A program may use at most 128 MiB of HBM per device.

v0:
```python
import jax
import jax.numpy as jnp
from jax import lax
from jax.sharding import PartitionSpec as P

SEQ = 256
layer_eps = 1e-06


def local(tokens, modulation, up_weight, up_bias, down_weight, down_bias):
    tok_dev = tokens.shape[0]
    first_tok = (lax.axis_index("row") * lax.axis_size("col") + lax.axis_index("col")) * tok_dev
    sample = first_tok // SEQ
    own_mods = lax.dynamic_slice_in_dim(modulation, sample, 1, 1)[:, 0]
    shift_vec = own_mods[0]
    scale_vec = own_mods[1]
    gate_vec = own_mods[2]
    average = jnp.mean(tokens, axis=1, keepdims=True)
    centred = tokens - average
    spread_sq = jnp.mean(centred * centred, axis=1, keepdims=True)
    normed = centred * lax.rsqrt(spread_sq + layer_eps)
    mixed = normed * (1.0 + scale_vec) + shift_vec
    columns = lax.all_to_all(mixed, "row", split_axis=1, concat_axis=0, tiled=True)
    partial_value = jnp.dot(
        lax.all_gather(columns, "col", axis=0, tiled=True),
        up_weight,
        precision=lax.Precision.HIGH,
        preferred_element_type=jnp.float32,
    )
    own_share = lax.psum_scatter(partial_value, "row", scatter_dimension=0, tiled=True)
    activated_share = jax.nn.gelu(own_share + up_bias, approximate=True)
    activated = lax.all_gather(activated_share, "row", axis=0, tiled=True)
    out_share = lax.psum_scatter(
        jnp.dot(
            activated, down_weight, precision=lax.Precision.HIGH, preferred_element_type=jnp.float32
        ),
        "col",
        scatter_dimension=0,
        tiled=True,
    )
    returned = lax.all_to_all(out_share, "row", split_axis=0, concat_axis=1, tiled=True)
    return tokens + gate_vec * (returned + down_bias)


def solution(mesh):
    in_specs = (
        P(("groups", "row", "col"), None),
        P(None, "groups", None),
        P("row", "col"),
        P("col"),
        P("col", "row"),
        P(),
    )
    out_specs = P(("groups", "row", "col"), None)
    return jax.shard_map(local, mesh=mesh, in_specs=in_specs, out_specs=out_specs, check_vma=False)
```

profile of v0, /device:TPU:0, one launch (start us, length us, event | category | flops | bytes accessed | tf_op | source)
XLA Modules:
  0.0 183.2 jit_solution(12808481648443348210)
XLA Ops:
  6.5 0.0 copy-start.2
  6.5 0.0 all-gather.3.cloned.1.call-start
  6.5 1.1 reduce_sum.18
  7.7 1.2 multiply_reduce_fusion
  8.9 0.8 fusion.7
  9.7 1.1 multiply_add_fusion.1
  10.8 10.2 %all_to_all.38 = f32[8,4,2048]{2,0,1:T(8,128)} all-to-all(f32[8,4,2048]{2,0,1:T(8,128)S(1)} %bitcast.16), channel_id=1, replica_groups=mesh['groups'=2,'row'=4,'col'=4] {'row'}, dimensions={1} | all-to-all | bytes 524288 | tf_op jit(solution)/shard_map/all_to_all | solution.py:23
  20.9 0.0 all-gather.3.cloned.1.call-update
  21.0 0.0 copy-start
  21.0 0.0 copy-start.1
  21.0 0.0 reduce-scatter.3.cloned.1.call-start
  21.0 28.7 %all-gather.3.cloned.1.call-done = f32[128,2048]{1,0:T(8,128)} async-done(((f32[32,2048]{1,0:T(8,128)}), f32[128,2048]{1,0:T(8,128)}) %all-gather.3.cloned.1.call-update) | async-done | bytes 1048592 | tf_op jit(solution)/shard_map/all_gather | solution.py:25
  49.8 17.7 %fusion.8 = f32[128,4096]{1,0:T(8,128)} fusion(f32[128,2048]{1,0:T(8,128)} %all-gather.3.cloned.1.call-done, f32[2048,4096]{1,0:T(8,128)} %param.8), kind=kOutput, calls=%fused_computation.15 | convolution fusion | flops 6442450944 | bytes 36700160 | tf_op jit(solution)/shard_map/dot_general | solution.py:24
  67.5 0.0 reduce-scatter.3.cloned.1.call-update
  67.5 0.0 all-gather.5.cloned.1.call-start
  67.6 31.0 %reduce-scatter.3.cloned.1.call-done = f32[32,4096]{1,0:T(8,128)} async-done(((f32[128,4096]{1,0:T(8,128)}), f32[32,4096]{1,0:T(8,128)}) %reduce-scatter.3.cloned.1.call-update) | async-done | bytes 524304 | tf_op jit(solution)/shard_map/reduce_scatter | solution.py:30
  98.6 0.0 copy-done.2
  98.6 2.0 %fusion.6 = f32[32,4096]{1,0:T(8,128)} fusion(f32[32,4096]{1,0:T(8,128)} %reduce-scatter.3.cloned.1.call-done, f32[4096]{0:T(1024)S(1)} %copy-done.2), kind=kLoop, calls=%fused_computation.7 | loop fusion | flops 1179648 | bytes 1064960 | tf_op jit(solution)/shard_map/mul | solution.py:31
  100.6 0.0 all-gather.5.cloned.1.call-update
  100.7 0.0 reduce-scatter.5.cloned.1.call-start
  100.7 22.7 %all-gather.5.cloned.1.call-done = f32[128,4096]{1,0:T(8,128)} async-done(((f32[32,4096]{1,0:T(8,128)}), f32[128,4096]{1,0:T(8,128)}) %all-gather.5.cloned.1.call-update) | async-done | bytes 2097168 | tf_op jit(solution)/shard_map/all_gather | solution.py:32
  123.4 15.8 %fusion.9 = f32[128,2048]{1,0:T(8,128)} fusion(f32[128,4096]{1,0:T(8,128)} %all-gather.5.cloned.1.call-done, f32[4096,2048]{1,0:T(8,128)} %param.10), kind=kOutput, calls=%fused_computation.16 | convolution fusion | flops 6442450944 | bytes 36700160 | tf_op jit(solution)/shard_map/dot_general | solution.py:34
  139.2 0.0 reduce-scatter.5.cloned.1.call-update
  139.2 27.3 %reduce-scatter.5.cloned.1.call-done = f32[32,2048]{1,0:T(8,128)} async-done(((f32[128,2048]{1,0:T(8,128)}), f32[32,2048]{1,0:T(8,128)}) %reduce-scatter.5.cloned.1.call-update) | async-done | bytes 262160 | tf_op jit(solution)/shard_map/reduce_scatter | solution.py:33
  166.5 9.4 %all_to_all.39 = f32[4,8,2048]{2,1,0:T(8,128)S(1)} all-to-all(f32[4,8,2048]{2,1,0:T(8,128)} %bitcast.18), channel_id=1, replica_groups=mesh['groups'=2,'row'=4,'col'=4] {'row'}, dimensions={0} | all-to-all | bytes 524288 | tf_op jit(solution)/shard_map/all_to_all | solution.py:41
  175.9 0.0 copy-done
  175.9 0.0 copy-done.1
  175.9 0.8 multiply_add_fusion
  (2 shorter events, 0.0 us)
Async XLA Ops:
  6.5 92.1 %copy-start.2 = (f32[4096]{0:T(1024)S(1)}, f32[4096]{0:T(1024)}, u32[]{:S(2)}) copy-start(f32[4096]{0:T(1024)} %param.9) | copy-start | bytes 49156
  6.5 43.2 %all-gather.3.cloned.1.call-start = ((), (), s32[]{:S(2)}) async-start(), calls=%async_computation.4 | async-start | bytes 1310720 | tf_op jit(solution)/shard_map/all_gather | solution.py:25
  21.0 154.9 %copy-start = (f32[8,8192]{1,0:T(8,128)S(1)}, f32[8,8192]{1,0:T(8,128)}, u32[]{:S(2)}) copy-start(f32[8,8192]{1,0:T(8,128)} %param.6) | copy-start | bytes 786436
  21.0 154.9 %copy-start.1 = (f32[8192]{0:T(1024)S(1)}, f32[8192]{0:T(1024)}, u32[]{:S(2)}) copy-start(f32[8192]{0:T(1024)} %param.11) | copy-start | bytes 98308
  21.0 77.6 %reduce-scatter.3.cloned.1.call-start = ((), (), s32[]{:S(2)}) async-start(), calls=%async_computation.5 | async-start | bytes 2621440 | tf_op jit(solution)/shard_map/reduce_scatter | solution.py:30
  67.5 55.9 %all-gather.5.cloned.1.call-start = ((), (), s32[]{:S(2)}) async-start(), calls=%async_computation.6 | async-start | bytes 2621440 | tf_op jit(solution)/shard_map/all_gather | solution.py:32
  100.7 65.9 %reduce-scatter.5.cloned.1.call-start = ((), (), s32[]{:S(2)}) async-start(), calls=%async_computation.7 | async-start | bytes 1310720 | tf_op jit(solution)/shard_map/reduce_scatter | solution.py:33
Sparse Core Ops, SparseCore 0:
  21.1 28.6 all-gather.2
  67.6 30.9 reduce-scatter.2
  100.8 22.5 all-gather.4
  139.3 27.1 reduce-scatter.4
where the time goes:
time: 184 us; the launch traced here: 183 us
  waiting for transfers between devices  110 us (60%)
  matrix products  33.5 us (18%)
  blocking collectives  19.6 us (11%)
  between operations  13.2 us (7%)
  other arithmetic  7.04 us (4%)
    reduce_scatter x1, waiting for transfers between devices, local(): lax.psum_scatter(partial_value, 'row', scatter_dimension=0, tiled=True)  31 us
    all_gather x1, waiting for transfers between devices, local(): lax.all_gather(columns, 'col', axis=0, tiled=True)  28.7 us
    reduce_scatter x1, waiting for transfers between devices, local(): lax.psum_scatter(jnp.dot(activated, down_weight, precision=lax.Precision....  27.3 us
    all_gather x1, waiting for transfers between devices, local(): activated = lax.all_gather(activated_share, 'row', axis=0, tiled=True)  22.7 us
    dot_general x1, matrix products, local(): jnp.dot(lax.all_gather(columns, 'col', axis=0, tiled=True), up_weight, pr...  17.7 us
    dot_general x1, matrix products, local(): jnp.dot(activated, down_weight, precision=lax.Precision.HIGH, preferred_e...  15.8 us
    all_to_all x1, blocking collectives, local(): lax.all_to_all(mixed, 'row', split_axis=1, concat_axis=0, tiled=True)  10.2 us
    all_to_all x1, blocking collectives, local(): lax.all_to_all(out_share, 'row', split_axis=0, concat_axis=1, tiled=True)  9.41 us
  transfers between devices with their start and end apart: 4, of which 4 were waited for; matrix products, arithmetic and copies ran while one was open for 0% of the time, Pallas kernels for 0%

commit v1 on v0

--- a/solution.py
+++ b/solution.py
@@ -29,7 +29,13 @@
     )
     own_share = lax.psum_scatter(partial_value, "row", scatter_dimension=0, tiled=True)
     activated_share = jax.nn.gelu(own_share + up_bias, approximate=True)
-    activated = lax.all_gather(activated_share, "row", axis=0, tiled=True)
+    size = lax.axis_size("row")
+    held, tiles = (activated_share, [activated_share])
+    for _ in range(size - 1):
+        held = lax.ppermute(held, "row", [(i, (i + 1) % size) for i in range(size)])
+        tiles.insert(0, held)
+    line = jnp.concatenate(tiles, axis=0)
+    activated = jnp.roll(line, (lax.axis_index("row") + 1) * activated_share.shape[0], axis=0)
     out_share = lax.psum_scatter(
         jnp.dot(
             activated, down_weight, precision=lax.Precision.HIGH, preferred_element_type=jnp.float32

time: 184 us -> 193 us (1.049)
  local copies, waits for them, and re-layouts: 0.02 us -> 4.99 us
  waiting for transfers between devices: 110 us -> 113 us
    ppermute x0 -> x3, waiting for transfers between devices: none -> 25.8 us  [local(): held = lax.ppermute(held, 'row', [(i, (i + 1) % size) for i in range(size)])]
    all_gather x1 -> x0, waiting for transfers between devices: 22.7 us -> none  [local(): activated = lax.all_gather(activated_share, 'row', axis=0, tiled=True)]
    unnamed x6 -> x14, local copies, waits for them, and re-layouts: 0.02 us -> 4.99 us
  transfers between devices with their start and end apart: 4 -> 6, of which waited for: 4 -> 6; matrix products, arithmetic and copies ran while one was open for 0% -> 0% of each run, Pallas kernels for 0% -> 0%
where the time goes in v1:
time: 193 us
  waiting for transfers between devices  113 us (59%)
  matrix products  33.5 us (17%)
  blocking collectives  19.6 us (10%)
  between operations  13.1 us (7%)
  other arithmetic  8.24 us (4%)
  local copies, waits for them, and re-layouts  4.99 us (3%)
    reduce_scatter x1, waiting for transfers between devices, local(): lax.psum_scatter(partial_value, 'row', scatter_dimension=0, tiled=True)  31 us
    all_gather x1, waiting for transfers between devices, local(): lax.all_gather(columns, 'col', axis=0, tiled=True)  28.7 us
    reduce_scatter x1, waiting for transfers between devices, local(): lax.psum_scatter(jnp.dot(activated, down_weight, precision=lax.Precision....  27.3 us
    ppermute x3, waiting for transfers between devices, local(): held = lax.ppermute(held, 'row', [(i, (i + 1) % size) for i in range(size)])  25.8 us
    dot_general x1, matrix products, local(): jnp.dot(lax.all_gather(columns, 'col', axis=0, tiled=True), up_weight, pr...  17.7 us
    dot_general x1, matrix products, local(): jnp.dot(activated, down_weight, precision=lax.Precision.HIGH, preferred_e...  15.8 us
    all_to_all x1, blocking collectives, local(): lax.all_to_all(mixed, 'row', split_axis=1, concat_axis=0, tiled=True)  10.2 us
    all_to_all x1, blocking collectives, local(): lax.all_to_all(out_share, 'row', split_axis=0, concat_axis=1, tiled=True)  9.41 us
  transfers between devices with their start and end apart: 6, of which 6 were waited for; matrix products, arithmetic and copies ran while one was open for 0% of the time, Pallas kernels for 0%

profile of v1, /device:TPU:0, one launch (start us, length us, event | category | flops | bytes accessed | tf_op | source)
XLA Modules:
  0.0 192.5 jit_solution(3850129601855439194)
XLA Ops:
  6.5 0.0 all-gather.2.cloned.1.call-start
  6.5 0.8 fusion.10
  7.4 1.1 reduce_sum.18
  8.5 1.2 multiply_reduce_fusion
  9.7 1.1 multiply_add_fusion.1
  10.8 10.2 %all_to_all.38 = f32[8,4,2048]{2,0,1:T(8,128)} all-to-all(f32[8,4,2048]{2,0,1:T(8,128)S(1)} %bitcast.15), channel_id=1, replica_groups=mesh['groups'=2,'row'=4,'col'=4] {'row'}, dimensions={1} | all-to-all | bytes 524288 | tf_op jit(solution)/shard_map/all_to_all | solution.py:23
  20.9 0.0 all-gather.2.cloned.1.call-update
  21.0 0.0 copy-start.2
  21.0 0.0 reduce-scatter.3.cloned.1.call-start
  21.0 28.7 %all-gather.2.cloned.1.call-done = f32[128,2048]{1,0:T(8,128)} async-done(((f32[32,2048]{1,0:T(8,128)}), f32[128,2048]{1,0:T(8,128)}) %all-gather.2.cloned.1.call-update) | async-done | bytes 1048592 | tf_op jit(solution)/shard_map/all_gather | solution.py:25
  49.8 17.7 %fusion.11 = f32[128,4096]{1,0:T(8,128)} fusion(f32[128,2048]{1,0:T(8,128)} %all-gather.2.cloned.1.call-done, f32[2048,4096]{1,0:T(8,128)} %param.8), kind=kOutput, calls=%fused_computation.26 | convolution fusion | flops 6442450944 | bytes 36700160 | tf_op jit(solution)/shard_map/dot_general | solution.py:24
  67.4 0.0 reduce-scatter.3.cloned.1.call-update
  67.5 0.0 reduce-scatter.5.cloned.1.call-start
  67.5 31.0 %reduce-scatter.3.cloned.1.call-done = f32[32,4096]{1,0:T(8,128)} async-done(((f32[128,4096]{1,0:T(8,128)}), f32[32,4096]{1,0:T(8,128)}) %reduce-scatter.3.cloned.1.call-update) | async-done | bytes 524304 | tf_op jit(solution)/shard_map/reduce_scatter | solution.py:30
  98.5 0.0 copy-done.2
  98.5 0.0 copy-start
  98.5 1.3 fusion.8
  99.8 0.1 collective-permute-start
  99.9 8.6 %collective-permute-done = f32[32,4096]{1,0:T(8,128)S(1)} collective-permute-done((f32[32,4096]{1,0:T(8,128)S(1)}, f32[32,4096]{1,0:T(8,128)S(1)}, u32[]{:S(2)}, u32[]{:S(2)}) %collective-permute-start) | collective-permute-done | bytes 524320 | tf_op jit(solution)/shard_map/ppermute | solution.py:35
  108.5 0.0 collective-permute-start.1
  108.5 8.6 %collective-permute-done.1 = f32[32,4096]{1,0:T(8,128)S(1)} collective-permute-done((f32[32,4096]{1,0:T(8,128)S(1)}, f32[32,4096]{1,0:T(8,128)S(1)}, u32[]{:S(2)}, u32[]{:S(2)}) %collective-permute-start.1) | collective-permute-done | bytes 524320 | tf_op jit(solution)/shard_map/ppermute | solution.py:35
  117.1 0.0 collective-permute-start.2
  117.1 8.6 %collective-permute-done.2 = f32[32,4096]{1,0:T(8,128)S(1)} collective-permute-done((f32[32,4096]{1,0:T(8,128)S(1)}, f32[32,4096]{1,0:T(8,128)S(1)}, u32[]{:S(2)}, u32[]{:S(2)}) %collective-permute-start.2) | collective-permute-done | bytes 524320 | tf_op jit(solution)/shard_map/ppermute | solution.py:35
  125.7 0.8 constant_dynamic-update-slice_fusion.7
  126.5 0.8 constant_dynamic-update-slice_fusion.6
  127.4 0.8 constant_dynamic-update-slice_fusion.5
  128.2 0.0 copy-done
  128.2 1.0 constant_dynamic-update-slice_fusion.4
  129.2 0.8 constant_dynamic-update-slice_fusion.3
  130.0 0.8 constant_dynamic-update-slice_fusion.2
  130.8 0.8 constant_dynamic-update-slice_fusion.1
  131.7 1.0 constant_dynamic-update-slice_fusion
  132.6 0.0 copy-start.1
  132.6 0.0 copy-start.3
  132.6 15.8 %fusion = f32[128,2048]{1,0:T(8,128)} fusion(f32[4096,2048]{1,0:T(8,128)} %param.10, f32[256,4096]{1,0:T(8,128)} %constant_dynamic-update-slice_fusion, s32[]{:T(128)S(6)} %select_n.17), kind=kOutput, calls=%fused_computation | convolution fusion | flops 6442450944 | bytes 36700164 | tf_op jit(solution)/shard_map/dot_general | solution.py:40
  148.5 0.0 reduce-scatter.5.cloned.1.call-update
  148.5 27.3 %reduce-scatter.5.cloned.1.call-done = f32[32,2048]{1,0:T(8,128)} async-done(((f32[128,2048]{1,0:T(8,128)}), f32[32,2048]{1,0:T(8,128)}) %reduce-scatter.5.cloned.1.call-update) | async-done | bytes 262160 | tf_op jit(solution)/shard_map/reduce_scatter | solution.py:39
  175.8 9.4 %all_to_all.39 = f32[4,8,2048]{2,1,0:T(8,128)S(1)} all-to-all(f32[4,8,2048]{2,1,0:T(8,128)} %bitcast.17), channel_id=1, replica_groups=mesh['groups'=2,'row'=4,'col'=4] {'row'}, dimensions={0} | all-to-all | bytes 524288 | tf_op jit(solution)/shard_map/all_to_all | solution.py:47
  185.2 0.0 copy-done.1
  185.2 0.0 copy-done.3
  185.2 0.8 multiply_add_fusion
  (2 shorter events, 0.0 us)
Async XLA Ops:
  6.5 43.2 %all-gather.2.cloned.1.call-start = ((), (), s32[]{:S(2)}) async-start(), calls=%async_computation.4 | async-start | bytes 1310720 | tf_op jit(solution)/shard_map/all_gather | solution.py:25
  21.0 77.6 %copy-start.2 = (f32[4096]{0:T(1024)S(1)}, f32[4096]{0:T(1024)}, u32[]{:S(2)}) copy-start(f32[4096]{0:T(1024)} %param.9) | copy-start | bytes 49156
  21.0 77.6 %reduce-scatter.3.cloned.1.call-start = ((), (), s32[]{:S(2)}) async-start(), calls=%async_computation.5 | async-start | bytes 2621440 | tf_op jit(solution)/shard_map/reduce_scatter | solution.py:30
  67.5 108.3 %reduce-scatter.5.cloned.1.call-start = ((), (), s32[]{:S(2)}) async-start(), calls=%async_computation.6 | async-start | bytes 1310720 | tf_op jit(solution)/shard_map/reduce_scatter | solution.py:39
  98.5 29.7 %copy-start = (f32[32,4096]{1,0:T(8,128)S(1)}, f32[32,4096]{1,0:T(8,128)}, u32[]{:S(2)}) copy-start(f32[32,4096]{1,0:T(8,128)} %reduce-scatter.3.cloned.1.call-done) | copy-start | bytes 1572868
  99.8 8.7 %collective-permute-start = (f32[32,4096]{1,0:T(8,128)S(1)}, f32[32,4096]{1,0:T(8,128)S(1)}, u32[]{:S(2)}, u32[]{:S(2)}) collective-permute-start(f32[32,4096]{1,0:T(8,128)S(1)} %fusion.8), channel_id=1, source_target_pairs={{0,4},{4,8},{8,12},{12,0},{1,5},{5,9},{9,13},{13,1},{2,6},{6,10},{... | collective-permute-start | bytes 1572872 | tf_op jit(solution)/shard_map/ppermute | solution.py:35
  108.5 8.6 %collective-permute-start.1 = (f32[32,4096]{1,0:T(8,128)S(1)}, f32[32,4096]{1,0:T(8,128)S(1)}, u32[]{:S(2)}, u32[]{:S(2)}) collective-permute-start(f32[32,4096]{1,0:T(8,128)S(1)} %collective-permute-done), channel_id=1, source_target_pairs={{0,4},{4,8},{8,12},{12,0},{1,5},{5,9},{9,13},{13,1},{2,6},{6,10},{... | collective-permute-start | bytes 1572872 | tf_op jit(solution)/shard_map/ppermute | solution.py:35
  117.1 8.6 %collective-permute-start.2 = (f32[32,4096]{1,0:T(8,128)S(1)}, f32[32,4096]{1,0:T(8,128)S(1)}, u32[]{:S(2)}, u32[]{:S(2)}) collective-permute-start(f32[32,4096]{1,0:T(8,128)S(1)} %collective-permute-done.1), channel_id=1, source_target_pairs={{0,4},{4,8},{8,12},{12,0},{1,5},{5,9},{9,13},{13,1},{2,6},{6,10},{... | collective-permute-start | bytes 1572872 | tf_op jit(solution)/shard_map/ppermute | solution.py:35
  132.6 52.6 %copy-start.1 = (f32[8,8192]{1,0:T(8,128)S(1)}, f32[8,8192]{1,0:T(8,128)}, u32[]{:S(2)}) copy-start(f32[8,8192]{1,0:T(8,128)} %param.6) | copy-start | bytes 786436
  132.6 52.6 %copy-start.3 = (f32[8192]{0:T(1024)S(1)}, f32[8192]{0:T(1024)}, u32[]{:S(2)}) copy-start(f32[8192]{0:T(1024)} %param.11) | copy-start | bytes 98308
Sparse Core Ops, SparseCore 0:
  21.1 28.6 all-gather.1
  67.6 30.9 reduce-scatter.2
  148.6 27.1 reduce-scatter.4
